TPU v7x, 256 devices: a whole 4x4x8 slice. The times are simulated.
256 devices in a mesh: dp: 16 (over x, y_hi, core), seq: 16 (over z, y_lo).
Axes of the slice: x: 4, y: 4 (y_hi: 2, y_lo: 2; y = y_hi * 2 + y_lo), z: 8, core: 2. Of those that a mesh axis runs over, the one named last changes fastest.
Arguments:
- queries: bfloat16 [40960, 768], P(('dp', 'seq')), may hold values from -8 to 8
- keys: bfloat16 [40960, 768], P(('dp', 'seq')), may hold values from -8 to 8
- values: bfloat16 [40960, 768], P(('dp', 'seq')), may hold values from -6 to 6
- frames: bfloat16 [40960, 768], P(('dp', 'seq')), may hold values from -4 to 4
- upstream: bfloat16 [40960, 768], P(('dp', 'seq')), may hold values from -6 to 6
- lengths: int32 [16], P('dp'), may hold values from 640 to 2560, as said below
- conv_kernel: bfloat16 [32, 768], replicated, may hold values from -1 to 1
Outputs:
- out: bfloat16 [40960, 768], P(('dp', 'seq'))
- query_grad: bfloat16 [40960, 768], P(('dp', 'seq'))
- key_grad: bfloat16 [40960, 768], P(('dp', 'seq'))
- value_grad: bfloat16 [40960, 768], P(('dp', 'seq'))
- frame_grad: bfloat16 [40960, 768], P(('dp', 'seq'))
- kernel_grad: float32 [32, 768], replicated
Inputs may be any that keep to these rules, and one draw needn't show every extreme that they name: `lengths`: one utterance has all 2560 frames live and another has 640.
All inputs are finite; a program needn't handle non-finite values.
Results may differ from a plain program's by a relative error of at most 0.0262.
Values may be sent and summed in bfloat16 or wider, within the bound.
No kernel may reach another device: no remote copies, remote signals or barrier semaphores. Data moves between devices by JAX's collectives and lax.ppermute only.
A program may use at most 128 MiB of HBM per device.

v0:
```python
import jax
import jax.numpy as jnp
from jax import lax
from jax.sharding import Mesh
from jax.sharding import PartitionSpec as P

HEAD_DIM = 64
KERNEL = 32
GROUPS = 4


def shifted(x, axis, by):
    count = lax.axis_size(axis)
    pairs = [(i, i + by) for i in range(count) if 0 <= i + by < count]
    return lax.ppermute(x, axis, pairs)


def butterfly_sum(x, axes):
    for axis in axes:
        count = lax.axis_size(axis)
        step = 1
        while step < count:
            x = x + lax.ppermute(x, axis, [(i, i ^ step) for i in range(count)])
            step = step * 2
    return x


def per_device(queries, keys, values, frames, upstream, lengths, conv_kernel):
    rows = queries.shape[0]
    channels = queries.shape[1]
    sub_count = lax.axis_size("sb")
    block_count_a = lax.axis_size("sa")
    group = channels // sub_count
    head_count = group // HEAD_DIM
    row_count = rows * sub_count
    span = row_count * block_count_a
    block_index = lax.axis_index("sa")
    group_index = lax.axis_index("sb")
    first_row = block_index * row_count
    length = lengths[0]
    score_scale = HEAD_DIM ** (-0.5)
    stacked = jnp.stack([queries, keys, values, frames, upstream])
    mixed = lax.all_to_all(
        stacked.reshape(5, rows, sub_count, group), "sb", 2, 1, tiled=True
    ).reshape(5, row_count, group)
    queries_b = mixed[0]
    frames_b = mixed[3]
    upstream_b = mixed[4]
    kv_all = lax.all_gather(jnp.concatenate([mixed[1], mixed[2]], axis=1), "sa", axis=0, tiled=True)
    key_all = kv_all[:, :group]
    value_all = kv_all[:, group:]
    key_block = row_count
    block_count = span // key_block
    key_blocks = key_all.reshape(block_count, key_block, head_count, HEAD_DIM)
    value_blocks = value_all.reshape(block_count, key_block, head_count, HEAD_DIM)
    block_starts = jnp.arange(block_count, dtype=jnp.int32) * key_block
    query_heads = queries_b.reshape(row_count, head_count, HEAD_DIM)

    def block_scores(key_part, block_start):
        scores = (
            jnp.einsum("thd,khd->htk", query_heads, key_part, preferred_element_type=jnp.float32)
            * score_scale
        )
        key_live = block_start + jnp.arange(key_part.shape[0], dtype=jnp.int32) < length
        return jnp.where(key_live[None, None, :], scores, -jnp.inf)

    def running_total(state_pair, block_items):
        running_top, total_sum = state_pair
        key_part, block_start = block_items
        scores = block_scores(key_part, block_start)
        higher = jnp.maximum(running_top, jnp.max(scores, axis=2))
        total_sum = total_sum * jnp.exp(running_top - higher) + jnp.sum(
            jnp.exp(scores - higher[:, :, None]), axis=2
        )
        return ((higher, total_sum), None)

    start_state = (
        jnp.full((head_count, row_count), -1e30, jnp.float32),
        jnp.zeros((head_count, row_count), jnp.float32),
    )
    (running_top, total_sum), unused = lax.scan(
        running_total, start_state, (key_blocks, block_starts)
    )
    log_total = running_top + jnp.log(total_sum)

    def attend_block(attend_acc, block_items):
        key_part, value_part, block_start = block_items
        prob_bf = jnp.exp(block_scores(key_part, block_start) - log_total[:, :, None]).astype(
            jnp.bfloat16
        )
        return (
            attend_acc
            + jnp.einsum("htk,khd->thd", prob_bf, value_part, preferred_element_type=jnp.float32),
            None,
        )

    attend_acc, unused = lax.scan(
        attend_block,
        jnp.zeros((row_count, head_count, HEAD_DIM), jnp.float32),
        (key_blocks, value_blocks, block_starts),
    )
    attended = attend_acc.reshape(row_count, group).astype(jnp.bfloat16)
    frame_live = (first_row + jnp.arange(row_count, dtype=jnp.int32) < length)[:, None]
    hidden = (frames_b.astype(jnp.float32) + attended.astype(jnp.float32)).astype(jnp.bfloat16)
    masked = jnp.where(frame_live, hidden, jnp.zeros_like(hidden))
    past_rows = shifted(masked[row_count - (KERNEL - 1) :], "sa", 1)
    extended = jnp.concatenate([past_rows, masked], axis=0).astype(jnp.float32)
    weights = lax.dynamic_slice_in_dim(conv_kernel, group_index * group, group, axis=1).astype(
        jnp.float32
    )
    conv_out = jnp.zeros((row_count, group), jnp.float32)
    for tap_index in range(KERNEL):
        conv_out = (
            conv_out
            + weights[tap_index]
            * extended[KERNEL - 1 - tap_index : KERNEL - 1 - tap_index + row_count]
        )
    sig_conv = jax.nn.sigmoid(conv_out)
    out = (hidden.astype(jnp.float32) + conv_out * sig_conv).astype(jnp.bfloat16)
    loss_grad = jnp.where(frame_live, upstream_b.astype(jnp.float32), 0.0)
    conv_grad = (loss_grad * sig_conv * (1.0 + conv_out * (1.0 - sig_conv))).astype(jnp.bfloat16)
    conv_float = conv_grad.astype(jnp.float32)
    kernel_part = jnp.stack(
        [
            jnp.sum(
                conv_float * extended[KERNEL - 1 - tap_index : KERNEL - 1 - tap_index + row_count],
                axis=0,
            )
            for tap_index in range(KERNEL)
        ]
    )
    future_rows = shifted(conv_grad[: KERNEL - 1], "sa", -1)
    ahead_rows = jnp.concatenate([conv_grad, future_rows], axis=0).astype(jnp.float32)
    back_conv = jnp.zeros((row_count, group), jnp.float32)
    for tap_index in range(KERNEL):
        back_conv = back_conv + weights[tap_index] * ahead_rows[tap_index : tap_index + row_count]
    frame_grad = (loss_grad + jnp.where(frame_live, back_conv, 0.0)).astype(jnp.bfloat16)
    grad_heads = frame_grad.reshape(row_count, head_count, HEAD_DIM)
    attended_heads = attended.reshape(row_count, head_count, HEAD_DIM)
    delta_rows = jnp.sum(
        grad_heads.astype(jnp.float32) * attended_heads.astype(jnp.float32), axis=2
    ).T

    def score_grads(key_part, value_part, block_start):
        soft_weights = jnp.exp(block_scores(key_part, block_start) - log_total[:, :, None])
        prob_grad = jnp.einsum(
            "thd,khd->htk", grad_heads, value_part, preferred_element_type=jnp.float32
        )
        score_grad = (soft_weights * (prob_grad - delta_rows[:, :, None])).astype(jnp.bfloat16)
        return (soft_weights.astype(jnp.bfloat16), score_grad)

    def gradient_block(query_acc, block_items):
        key_part, value_part, block_start = block_items
        prob_bf, score_grad = score_grads(key_part, value_part, block_start)
        query_acc = query_acc + jnp.einsum(
            "htk,khd->thd", score_grad, key_part, preferred_element_type=jnp.float32
        )
        key_term = (
            jnp.einsum("htk,thd->khd", score_grad, query_heads, preferred_element_type=jnp.float32)
            * score_scale
        )
        value_term = jnp.einsum(
            "htk,thd->khd", prob_bf, grad_heads, preferred_element_type=jnp.float32
        )
        grad_terms = jnp.concatenate(
            [key_term.reshape(key_block, group), value_term.reshape(key_block, group)], axis=1
        )
        return (query_acc, grad_terms)

    query_acc, grad_terms = lax.scan(
        gradient_block,
        jnp.zeros((row_count, head_count, HEAD_DIM), jnp.float32),
        (key_blocks, value_blocks, block_starts),
    )
    own_rows = lax.psum_scatter(
        grad_terms.reshape(span, 2 * group).astype(jnp.bfloat16),
        "sa",
        scatter_dimension=0,
        tiled=True,
    ).astype(jnp.float32)
    key_grad = own_rows[:, :group].astype(jnp.bfloat16)
    value_grad = own_rows[:, group:].astype(jnp.bfloat16)
    query_grad = (query_acc * score_scale).reshape(row_count, group).astype(jnp.bfloat16)
    kernel_full = lax.dynamic_update_slice_in_dim(
        jnp.zeros((KERNEL, channels), jnp.float32), kernel_part, group_index * group, axis=1
    )
    kernel_total = butterfly_sum(kernel_full, ("sb", "sa", "dp"))
    kernel_grad = kernel_total / lax.axis_size("dp")
    results = jnp.stack([out, query_grad, key_grad, value_grad, frame_grad])
    spread = lax.all_to_all(
        results.reshape(5, sub_count, rows, 1, group), "sb", 1, 3, tiled=True
    ).reshape(5, rows, channels)
    return (spread[0], spread[1], spread[2], spread[3], spread[4], kernel_grad)


def solution(mesh):
    seq_count = mesh.shape["seq"]
    split_mesh = Mesh(
        mesh.devices.reshape(mesh.shape["dp"], seq_count // GROUPS, GROUPS), ("dp", "sa", "sb")
    )
    rows_spec = P(("dp", "sa", "sb"), None)
    placed = (rows_spec, rows_spec, rows_spec, rows_spec, rows_spec, P("dp"), P())
    return jax.shard_map(
        per_device,
        mesh=split_mesh,
        in_specs=placed,
        out_specs=(rows_spec, rows_spec, rows_spec, rows_spec, rows_spec, P()),
        check_vma=False,
    )
```

profile of v0, /device:TPU:2, one launch (start us, length us, event | category | flops | bytes accessed | tf_op | source)
XLA Modules:
  0.0 392.6 jit_solution(232273346341479808)
XLA Ops:
  12.7 24.6 %all_to_all.30 = bf16[5,160,4,192]{3,1,0,2:T(8,128)(2,1)S(1)} all-to-all(bf16[5,160,4,192]{3,1,0,2:T(8,128)(2,1)S(1)} %copy.80), channel_id=1, replica_groups=mesh['dp'=16,'sa'=4,'sb'=4] {'sb'}, dimensions={2} | all-to-all | bytes 2457600 | tf_op jit(solution)/shard_map/all_to_all | solution.py:43
  41.8 47.3 %all-gather.2.cloned.1.call-done = bf16[2560,384]{1,0:T(8,128)(2,1)} async-done(((bf16[640,384]{1,0:T(8,128)(2,1)}), bf16[2560,384]{1,0:T(8,128)(2,1)}) %all-gather.2.cloned.1.call-update) | async-done | bytes 1966096 | tf_op jit(solution)/shard_map/all_gather | solution.py:49
  89.1 2.3 fusion.111
  91.4 1.4 copy.82
  92.8 1.9 reshape.121
  95.8 40.8 %while.37 = (s32[]{:T(128)}, f32[3,640]{1,0:T(4,128)S(1)}, f32[3,640]{1,0:T(4,128)S(1)}, s32[4]{0:T(128)}, s32[]{:T(128)}, /*index=5*/bf16[4,640,3,64]{1,3,2,0:T...) while((s32[]{:T(128)}, f32[3,640]{1,0:T(4,128)S(1)}, f32[3,640]{1,0:T(4,128)S(1)}, ...), condition=%wide.region_3.4_spmd.clone, body=%wide.region_0.3_spmd.clone.sunk | while | flops 165898880 | bytes 10424316 | solution.py:81
  98.4 4.1 %bitcast_reduce_fusion.2 = (f32[3,640]{1,0:T(4,128)S(1)}, f32[3,640,640]{2,1,0:T(8,128)}) fusion(pred[640]{0:T(1024)(128)(4,1)S(1)} %add_compare_fusion.7, bf16[640,3,64]{0,2,1:T(8,128)(2,1)S(1)} %get-tuple-element.670, bf16[4,640,3,64]{1,3,2,0:T(8,128)(2,1)} %get-tuple-element.669, s32[]{:T(128)} %get-tuple-element.655), kind=kOutput, calls=%fused_computation.1.clone.1 | convolution fusion | flops 160970880 | bytes 5415552 | tf_op jit(solution)/shard_map/while/body/eval_jaxpr/thd,khd->htk/dot_general | solution.py:61
  102.5 3.4 fusion.146
  108.6 4.1 %bitcast_reduce_fusion.2 = (f32[3,640]{1,0:T(4,128)S(1)}, f32[3,640,640]{2,1,0:T(8,128)}) fusion(pred[640]{0:T(1024)(128)(4,1)S(1)} %add_compare_fusion.7, bf16[640,3,64]{0,2,1:T(8,128)(2,1)S(1)} %get-tuple-element.670, bf16[4,640,3,64]{1,3,2,0:T(8,128)(2,1)} %get-tuple-element.669, s32[]{:T(128)} %get-tuple-element.655), kind=kOutput, calls=%fused_computation.1.clone.1 | convolution fusion | flops 160970880 | bytes 5415552 | tf_op jit(solution)/shard_map/while/body/eval_jaxpr/thd,khd->htk/dot_general | solution.py:61
  112.7 3.4 fusion.146
  118.8 4.1 %bitcast_reduce_fusion.2 = (f32[3,640]{1,0:T(4,128)S(1)}, f32[3,640,640]{2,1,0:T(8,128)}) fusion(pred[640]{0:T(1024)(128)(4,1)S(1)} %add_compare_fusion.7, bf16[640,3,64]{0,2,1:T(8,128)(2,1)S(1)} %get-tuple-element.670, bf16[4,640,3,64]{1,3,2,0:T(8,128)(2,1)} %get-tuple-element.669, s32[]{:T(128)} %get-tuple-element.655), kind=kOutput, calls=%fused_computation.1.clone.1 | convolution fusion | flops 160970880 | bytes 5415552 | tf_op jit(solution)/shard_map/while/body/eval_jaxpr/thd,khd->htk/dot_general | solution.py:61
  123.0 3.4 fusion.146
  129.0 4.1 %bitcast_reduce_fusion.2 = (f32[3,640]{1,0:T(4,128)S(1)}, f32[3,640,640]{2,1,0:T(8,128)}) fusion(pred[640]{0:T(1024)(128)(4,1)S(1)} %add_compare_fusion.7, bf16[640,3,64]{0,2,1:T(8,128)(2,1)S(1)} %get-tuple-element.670, bf16[4,640,3,64]{1,3,2,0:T(8,128)(2,1)} %get-tuple-element.669, s32[]{:T(128)} %get-tuple-element.655), kind=kOutput, calls=%fused_computation.1.clone.1 | convolution fusion | flops 160970880 | bytes 5415552 | tf_op jit(solution)/shard_map/while/body/eval_jaxpr/thd,khd->htk/dot_general | solution.py:61
  133.2 3.4 fusion.146
  138.2 24.5 %while.38 = (s32[]{:T(128)}, f32[640,3,64]{0,2,1:T(8,128)}, bf16[4,640,3,64]{1,3,2,0:T(8,128)(2,1)S(1)}, s32[4]{0:T(128)}, s32[]{:T(128)}, /*index=5*/bf16[4,640...) while((s32[]{:T(128)}, f32[640,3,64]{0,2,1:T(8,128)}, ...), condition=%wide.region_5.6_spmd.clone, body=%wide.region_4.5_spmd.clone.sunk | while | flops 319735040 | bytes 1733379 | solution.py:97
  140.8 3.4 fusion.151
  146.8 3.6 fusion.151
  152.9 3.6 fusion.151
  159.1 3.6 fusion.151
  165.3 5.2 %collective-permute-start = (bf16[31,192]{1,0:T(8,128)(2,1)S(1)}, bf16[31,192]{1,0:T(8,128)(2,1)S(1)}, u32[]{:S(2)}, u32[]{:S(2)}) collective-permute-start(bf16[31,192]{1,0:T(8,128)(2,1)S(1)} %slice.531), channel_id=1, source_target_pairs={{0,4},{4,8},{8,12},{1,5},{5,9},{9,13},{2,6},{6,10},{10,14},{3,7},{... | collective-permute-start | bytes 35720 | tf_op jit(solution)/shard_map/ppermute | solution.py:15
  172.1 7.1 %fusion.71 = (f32[192]{0:T(256)}, f32[192]{0:T(256)}, f32[192]{0:T(256)}, f32[192]{0:T(256)}, f32[192]{0:T(256)}, /*index=5*/f32[192]{0:T(256)}, f32[192]{0:T(25...) fusion(f32[671,192]{1,0:T(8,128)S(1)} %maximum_convert_fusion, ...), kind=kLoop, calls=%fused_computation.113 | loop fusion | flops 13636224 | bytes 16750720 | tf_op jit(solution)/shard_map/reduce_sum | solution.py:125
  180.5 5.6 %collective-permute-done.1 = bf16[31,192]{1,0:T(8,128)(2,1)S(1)} collective-permute-done((bf16[31,192]{1,0:T(8,128)(2,1)S(1)}, bf16[31,192]{1,0:T(8,128)(2,1)S(1)}, u32[]{:S(2)}, u32[]{:S(2)}) %collective-permute-start.1) | collective-permute-done | bytes 11936 | tf_op jit(solution)/shard_map/ppermute | solution.py:15
  186.2 3.1 fusion.75
  191.2 70.0 %while.39 = (s32[]{:T(128)}, f32[640,3,64]{0,2,1:T(8,128)}, bf16[4,640,384]{2,1,0:T(8,128)(2,1)}, bf16[4,640,3,64]{1,3,2,0:T(8,128)(2,1)}, s32[4]{0:T(128)}, /*i...) while((s32[]{:T(128)}, f32[640,3,64]{0,2,1:T(8,128)}, ...), condition=%wide.region_8.9_spmd.clone, body=%wide.region_7.8_spmd.clone.sunk | while | flops 800195840 | bytes 28292124 | solution.py:170
  191.2 1.8 fusion.162
  195.7 2.7 multiply_convert_fusion.3
  199.3 2.3 fusion.164
  202.4 2.0 copy.135
  204.4 1.8 constant_dynamic-update-slice_fusion.12
  206.3 2.3 fusion.163
  208.6 1.8 fusion.162
  213.0 2.7 multiply_convert_fusion.3
  216.6 2.3 fusion.164
  219.7 2.0 copy.135
  221.8 1.9 constant_dynamic-update-slice_fusion.12
  223.6 2.5 fusion.163
  226.1 1.8 fusion.162
  230.6 2.7 multiply_convert_fusion.3
  234.2 2.3 fusion.164
  237.3 2.0 copy.135
  239.3 1.9 constant_dynamic-update-slice_fusion.12
  241.2 2.5 fusion.163
  243.7 1.8 fusion.162
  248.1 2.7 multiply_convert_fusion.3
  251.7 2.3 fusion.164
  254.8 2.0 copy.135
  256.9 1.9 constant_dynamic-update-slice_fusion.12
  258.7 2.5 fusion.163
  261.2 2.9 fusion.70
  264.8 44.9 %reduce-scatter.2.cloned.1.call-done = bf16[640,384]{1,0:T(8,128)(2,1)} async-done(((bf16[2560,384]{1,0:T(8,128)(2,1)}), bf16[640,384]{1,0:T(8,128)(2,1)}) %reduce-scatter.2.cloned.1.call-update) | async-done | bytes 491536 | tf_op jit(solution)/shard_map/reduce_scatter | solution.py:175
  312.4 3.6 all-to-all-start.1
  316.8 2.4 collective-permute-start.2
  319.2 19.0 %collective-permute-done.2 = f32[32,768]{1,0:T(8,128)S(1)} collective-permute-done((f32[32,768]{1,0:T(8,128)S(1)}, f32[32,768]{1,0:T(8,128)S(1)}, u32[]{:S(2)}, u32[]{:S(2)}) %collective-permute-start.2) | collective-permute-done | bytes 98336 | tf_op jit(solution)/shard_map/ppermute | solution.py:23
  338.7 1.5 collective-permute-start.3
  340.2 3.2 collective-permute-done.3
  343.5 2.5 collective-permute-start.4
  345.9 4.4 %collective-permute-done.4 = f32[32,768]{1,0:T(8,128)S(1)} collective-permute-done((f32[32,768]{1,0:T(8,128)S(1)}, f32[32,768]{1,0:T(8,128)S(1)}, u32[]{:S(2)}, u32[]{:S(2)}) %collective-permute-start.4) | collective-permute-done | bytes 98336 | tf_op jit(solution)/shard_map/ppermute | solution.py:23
  350.3 2.5 collective-permute-start.5
  352.8 7.1 %collective-permute-done.5 = f32[32,768]{1,0:T(8,128)S(1)} collective-permute-done((f32[32,768]{1,0:T(8,128)S(1)}, f32[32,768]{1,0:T(8,128)S(1)}, u32[]{:S(2)}, u32[]{:S(2)}) %collective-permute-start.5) | collective-permute-done | bytes 98336 | tf_op jit(solution)/shard_map/ppermute | solution.py:23
  361.3 3.2 collective-permute-start.7
  364.5 3.3 collective-permute-done.7
  368.3 4.2 %collective-permute-done.8 = f32[32,768]{1,0:T(8,128)S(1)} collective-permute-done((f32[32,768]{1,0:T(8,128)S(1)}, f32[32,768]{1,0:T(8,128)S(1)}, u32[]{:S(2)}, u32[]{:S(2)}) %collective-permute-start.8) | collective-permute-done | bytes 98336 | tf_op jit(solution)/shard_map/ppermute | solution.py:23
  372.5 2.2 collective-permute-start.9
  374.7 4.0 %collective-permute-done.9 = f32[32,768]{1,0:T(8,128)S(1)} collective-permute-done((f32[32,768]{1,0:T(8,128)S(1)}, f32[32,768]{1,0:T(8,128)S(1)}, u32[]{:S(2)}, u32[]{:S(2)}) %collective-permute-start.9) | collective-permute-done | bytes 98336 | tf_op jit(solution)/shard_map/ppermute | solution.py:23
  (220 shorter events, 70.5 us)
Async XLA Ops:
  7.2 4.1 %copy-start.8 = (bf16[160,768]{1,0:T(8,128)(2,1)S(1)}, bf16[160,768]{1,0:T(8,128)(2,1)}, u32[]{:S(2)}) copy-start(bf16[160,768]{1,0:T(8,128)(2,1)} %param.16) | copy-start | bytes 737284
  7.2 4.4 %copy-start.9 = (bf16[160,768]{1,0:T(8,128)(2,1)S(1)}, bf16[160,768]{1,0:T(8,128)(2,1)}, u32[]{:S(2)}) copy-start(bf16[160,768]{1,0:T(8,128)(2,1)} %param.17) | copy-start | bytes 737284
  7.2 81.9 %all-gather.2.cloned.1.call-start = ((), (), s32[]{:S(2)}) async-start(), calls=%async_computation.3 | async-start | bytes 2457600 | tf_op jit(solution)/shard_map/all_gather | solution.py:49
  37.4 127.7 %copy-start.3 = (bf16[1,4,160,1,192]{4,2,0,1,3:T(8,128)(2,1)}, bf16[1,4,160,1,192]{4,2,0,1,3:T(8,128)(2,1)S(1)}, u32[]{:S(2)}) copy-start(bf16[1,4,160,1,192]{4,2,0,1,3:T(8,128)(2,1)S(1)} %get-tuple-element.447) | copy-start | bytes 737284
  38.5 271.2 %reduce-scatter.2.cloned.1.call-start = ((), (), s32[]{:S(2)}) async-start(), calls=%async_computation.4 | async-start | bytes 2457600 | tf_op jit(solution)/shard_map/reduce_scatter | solution.py:175
  40.6 1.2 copy-start.10
  162.7 1.0 copy-start.7
  163.7 8.2 %copy-start.11 = (f32[1,192]{1,0:T(1,128)S(1)}, f32[1,192]{1,0:T(1,128)}, u32[]{:S(2)}) copy-start(f32[1,192]{1,0:T(1,128)} %get-tuple-element.451) | copy-start | bytes 2308
  163.7 8.2 %copy-start.12 = (f32[1,192]{1,0:T(1,128)S(1)}, f32[1,192]{1,0:T(1,128)}, u32[]{:S(2)}) copy-start(f32[1,192]{1,0:T(1,128)} %get-tuple-element.452) | copy-start | bytes 2308
  163.7 8.3 %copy-start.13 = (f32[1,192]{1,0:T(1,128)S(1)}, f32[1,192]{1,0:T(1,128)}, u32[]{:S(2)}) copy-start(f32[1,192]{1,0:T(1,128)} %get-tuple-element.453) | copy-start | bytes 2308
  163.7 8.3 %copy-start.14 = (f32[1,192]{1,0:T(1,128)S(1)}, f32[1,192]{1,0:T(1,128)}, u32[]{:S(2)}) copy-start(f32[1,192]{1,0:T(1,128)} %get-tuple-element.454) | copy-start | bytes 2308
  163.7 8.3 %copy-start.15 = (f32[1,192]{1,0:T(1,128)S(1)}, f32[1,192]{1,0:T(1,128)}, u32[]{:S(2)}) copy-start(f32[1,192]{1,0:T(1,128)} %get-tuple-element.455) | copy-start | bytes 2308
  163.7 8.3 %copy-start.16 = (f32[1,192]{1,0:T(1,128)S(1)}, f32[1,192]{1,0:T(1,128)}, u32[]{:S(2)}) copy-start(f32[1,192]{1,0:T(1,128)} %get-tuple-element.456) | copy-start | bytes 2308
  163.7 8.3 %copy-start.17 = (f32[1,192]{1,0:T(1,128)S(1)}, f32[1,192]{1,0:T(1,128)}, u32[]{:S(2)}) copy-start(f32[1,192]{1,0:T(1,128)} %get-tuple-element.457) | copy-start | bytes 2308
  163.7 8.3 %copy-start.18 = (f32[1,192]{1,0:T(1,128)S(1)}, f32[1,192]{1,0:T(1,128)}, u32[]{:S(2)}) copy-start(f32[1,192]{1,0:T(1,128)} %get-tuple-element.458) | copy-start | bytes 2308
  163.7 8.3 %copy-start.19 = (f32[1,192]{1,0:T(1,128)S(1)}, f32[1,192]{1,0:T(1,128)}, u32[]{:S(2)}) copy-start(f32[1,192]{1,0:T(1,128)} %get-tuple-element.459) | copy-start | bytes 2308
  163.7 8.3 %copy-start.20 = (f32[1,192]{1,0:T(1,128)S(1)}, f32[1,192]{1,0:T(1,128)}, u32[]{:S(2)}) copy-start(f32[1,192]{1,0:T(1,128)} %get-tuple-element.460) | copy-start | bytes 2308
  163.7 8.3 %copy-start.21 = (f32[1,192]{1,0:T(1,128)S(1)}, f32[1,192]{1,0:T(1,128)}, u32[]{:S(2)}) copy-start(f32[1,192]{1,0:T(1,128)} %get-tuple-element.461) | copy-start | bytes 2308
  163.8 8.3 %copy-start.22 = (f32[1,192]{1,0:T(1,128)S(1)}, f32[1,192]{1,0:T(1,128)}, u32[]{:S(2)}) copy-start(f32[1,192]{1,0:T(1,128)} %get-tuple-element.462) | copy-start | bytes 2308
  163.8 8.3 %copy-start.23 = (f32[1,192]{1,0:T(1,128)S(1)}, f32[1,192]{1,0:T(1,128)}, u32[]{:S(2)}) copy-start(f32[1,192]{1,0:T(1,128)} %get-tuple-element.463) | copy-start | bytes 2308
  163.8 8.3 %copy-start.24 = (f32[1,192]{1,0:T(1,128)S(1)}, f32[1,192]{1,0:T(1,128)}, u32[]{:S(2)}) copy-start(f32[1,192]{1,0:T(1,128)} %get-tuple-element.464) | copy-start | bytes 2308
  163.8 8.3 %copy-start.25 = (f32[1,192]{1,0:T(1,128)S(1)}, f32[1,192]{1,0:T(1,128)}, u32[]{:S(2)}) copy-start(f32[1,192]{1,0:T(1,128)} %get-tuple-element.465) | copy-start | bytes 2308
  163.8 8.3 %copy-start.26 = (f32[1,192]{1,0:T(1,128)S(1)}, f32[1,192]{1,0:T(1,128)}, u32[]{:S(2)}) copy-start(f32[1,192]{1,0:T(1,128)} %get-tuple-element.466) | copy-start | bytes 2308
  163.8 8.3 %copy-start.27 = (f32[1,192]{1,0:T(1,128)S(1)}, f32[1,192]{1,0:T(1,128)}, u32[]{:S(2)}) copy-start(f32[1,192]{1,0:T(1,128)} %get-tuple-element.467) | copy-start | bytes 2308
  163.8 8.3 %copy-start.28 = (f32[1,192]{1,0:T(1,128)S(1)}, f32[1,192]{1,0:T(1,128)}, u32[]{:S(2)}) copy-start(f32[1,192]{1,0:T(1,128)} %get-tuple-element.468) | copy-start | bytes 2308
  165.1 6.4 %copy-start.1 = (f32[640,192]{1,0:T(8,128)}, f32[640,192]{1,0:T(8,128)S(1)}, u32[]{:S(2)}) copy-start(f32[640,192]{1,0:T(8,128)S(1)} %copy.87) | copy-start | bytes 1474564
  165.3 6.5 %collective-permute-start = (bf16[31,192]{1,0:T(8,128)(2,1)S(1)}, bf16[31,192]{1,0:T(8,128)(2,1)S(1)}, u32[]{:S(2)}, u32[]{:S(2)}) collective-permute-start(bf16[31,192]{1,0:T(8,128)(2,1)S(1)} %slice.531), channel_id=1, source_target_pairs={{0,4},{4,8},{8,12},{1,5},{5,9},{9,13},{2,6},{6,10},{10,14},{3,7},{... | collective-permute-start | bytes 35720 | tf_op jit(solution)/shard_map/ppermute | solution.py:15
  179.2 10.2 %copy-start.2 = (bf16[640,192]{1,0:T(8,128)(2,1)}, bf16[640,192]{1,0:T(8,128)(2,1)S(1)}, u32[]{:S(2)}) copy-start(bf16[640,192]{1,0:T(8,128)(2,1)S(1)} %get-tuple-element.432) | copy-start | bytes 737284
  179.2 6.9 %collective-permute-start.1 = (bf16[31,192]{1,0:T(8,128)(2,1)S(1)}, bf16[31,192]{1,0:T(8,128)(2,1)S(1)}, u32[]{:S(2)}, u32[]{:S(2)}) collective-permute-start(bf16[31,192]{1,0:T(8,128)(2,1)S(1)} %slice.596), channel_id=1, source_target_pairs={{4,0},{8,4},{12,8},{5,1},{9,5},{13,9},{6,2},{10,6},{14,10},{7,3},{... | collective-permute-start | bytes 35720 | tf_op jit(solution)/shard_map/ppermute | solution.py:15
  186.2 4.0 %copy-start.6 = (f32[640,3,64]{0,2,1:T(8,128)S(1)}, f32[640,3,64]{0,2,1:T(8,128)}, u32[]{:S(2)}) copy-start(f32[640,3,64]{0,2,1:T(8,128)} %get-tuple-element.146) | copy-start | bytes 1474564
  189.3 1.9 copy-start.4
  261.2 2.9 copy-start
  264.2 46.8 %copy-start.5 = (bf16[640,192]{1,0:T(8,128)(2,1)S(1)}, bf16[640,192]{1,0:T(8,128)(2,1)}, u32[]{:S(2)}) copy-start(bf16[640,192]{1,0:T(8,128)(2,1)} %copy-done.4) | copy-start | bytes 737284
  312.3 3.7 copy-start.29
  312.3 3.7 copy-start.30
  312.3 3.8 copy-start.31
  312.3 3.8 copy-start.32
  312.3 3.8 copy-start.33
  312.3 3.8 copy-start.34
  312.3 3.8 copy-start.35
  312.3 3.8 copy-start.36
  312.3 3.8 copy-start.37
  312.3 3.8 copy-start.38
  312.4 3.8 copy-start.39
  312.4 3.8 copy-start.40
  312.4 3.8 copy-start.41
  312.4 3.8 copy-start.42
  312.4 3.8 copy-start.43
  312.4 3.8 copy-start.44
  312.4 3.8 copy-start.45
  312.4 3.8 copy-start.46
  312.4 66.9 %all-to-all-start.1 = ((bf16[5,4,160,1,192]{4,2,3,0,1:T(8,128)(2,1)}), bf16[5,4,160,1,192]{4,2,3,0,1:T(8,128)(2,1)S(1)}, u32[]{:S(2)}, u32[]{:S(2)}) async-start(bf16[5,4,160,1,192]{4,2,3,0,1:T(8,128)(2,1)} %copy.93), calls=%async_computation.2 | async-start | bytes 3276800 | tf_op jit(solution)/shard_map/all_to_all | solution.py:190
  316.8 21.4 %collective-permute-start.2 = (f32[32,768]{1,0:T(8,128)S(1)}, f32[32,768]{1,0:T(8,128)S(1)}, u32[]{:S(2)}, u32[]{:S(2)}) collective-permute-start(f32[32,768]{1,0:T(8,128)S(1)} %dynamic_update_slice.9), channel_id=1, source_target_pairs={{0,1},{1,0},{2,3},{3,2},{4,5},{5,4},{6,7},{7,6},{8,9},{9,8},{10,11... | collective-permute-start | bytes 294920 | tf_op jit(solution)/shard_map/ppermute | solution.py:23
  338.7 4.7 %collective-permute-start.3 = (f32[32,768]{1,0:T(8,128)S(1)}, f32[32,768]{1,0:T(8,128)S(1)}, u32[]{:S(2)}, u32[]{:S(2)}) collective-permute-start(f32[32,768]{1,0:T(8,128)S(1)} %add.364), channel_id=1, source_target_pairs={{0,2},{1,3},{2,0},{3,1},{4,6},{5,7},{6,4},{7,5},{8,10},{9,11},{10,... | collective-permute-start | bytes 294920 | tf_op jit(solution)/shard_map/ppermute | solution.py:23
  343.5 6.8 %collective-permute-start.4 = (f32[32,768]{1,0:T(8,128)S(1)}, f32[32,768]{1,0:T(8,128)S(1)}, u32[]{:S(2)}, u32[]{:S(2)}) collective-permute-start(f32[32,768]{1,0:T(8,128)S(1)} %add.365), channel_id=1, source_target_pairs={{0,4},{4,0},{8,12},{12,8},{1,5},{5,1},{9,13},{13,9},{2,6},{6,2},{1... | collective-permute-start | bytes 294920 | tf_op jit(solution)/shard_map/ppermute | solution.py:23
  350.3 9.6 %collective-permute-start.5 = (f32[32,768]{1,0:T(8,128)S(1)}, f32[32,768]{1,0:T(8,128)S(1)}, u32[]{:S(2)}, u32[]{:S(2)}) collective-permute-start(f32[32,768]{1,0:T(8,128)S(1)} %add.366), channel_id=1, source_target_pairs={{0,8},{4,12},{8,0},{12,4},{1,9},{5,13},{9,1},{13,5},{2,10},{6,14},... | collective-permute-start | bytes 294920 | tf_op jit(solution)/shard_map/ppermute | solution.py:23
  359.9 1.4 collective-permute-start.6
  361.3 6.4 %collective-permute-start.7 = (f32[32,768]{1,0:T(8,128)S(1)}, f32[32,768]{1,0:T(8,128)S(1)}, u32[]{:S(2)}, u32[]{:S(2)}) collective-permute-start(f32[32,768]{1,0:T(8,128)S(1)} %add.368), channel_id=1, source_target_pairs={{0,32},{16,48},{32,0},{48,16},{64,96},{80,112},{96,64},{112,80},{1... | collective-permute-start | bytes 294920 | tf_op jit(solution)/shard_map/ppermute | solution.py:23
  367.8 4.7 %collective-permute-start.8 = (f32[32,768]{1,0:T(8,128)S(1)}, f32[32,768]{1,0:T(8,128)S(1)}, u32[]{:S(2)}, u32[]{:S(2)}) collective-permute-start(f32[32,768]{1,0:T(8,128)S(1)} %add.369), channel_id=1, source_target_pairs={{0,64},{16,80},{32,96},{48,112},{64,0},{80,16},{96,32},{112,48},{1... | collective-permute-start | bytes 294920 | tf_op jit(solution)/shard_map/ppermute | solution.py:23
  372.5 6.2 %collective-permute-start.9 = (f32[32,768]{1,0:T(8,128)S(1)}, f32[32,768]{1,0:T(8,128)S(1)}, u32[]{:S(2)}, u32[]{:S(2)}) collective-permute-start(f32[32,768]{1,0:T(8,128)S(1)} %add.370), channel_id=1, source_target_pairs={{0,128},{16,144},{32,160},{48,176},{64,192},{80,208},{96,224},{112... | collective-permute-start | bytes 294920 | tf_op jit(solution)/shard_map/ppermute | solution.py:23
Sparse Core Ops, SparseCore 0:
  38.6 50.4 all-gather.1
  261.3 48.2 reduce-scatter.1
where the time goes:
time: 395 us; the launch traced here: 393 us
  waiting for transfers between devices  145 us (37%)
  matrix products  71.1 us (18%)
  local copies, waits for them, and re-layouts  59.1 us (15%)
  other arithmetic  52.1 us (13%)
  starting transfers between devices  25 us (6%)
  blocking collectives  24.6 us (6%)
  between operations  15.7 us (4%)
    all_gather x1, waiting for transfers between devices, per_device(): lax.all_gather(jnp.concatenate([mixed[1], mixed[2]], axis=1), 'sa', axis=...  47.3 us
    ppermute x8, waiting for transfers between devices, butterfly_sum(): x = x + lax.ppermute(x, axis, [(i, i ^ step) for i in range(count)])  46.5 us
    reduce_scatter x1, waiting for transfers between devices, per_device(): lax.psum_scatter(grad_terms.reshape(span, 2 * group).astype(jnp.bfloat16)...  44.9 us
    all_to_all x1, blocking collectives, per_device(): lax.all_to_all(stacked.reshape(5, rows, sub_count, group), 'sb', 2, 1, ti...  24.6 us
    dot_general x8, matrix products, block_scores(): jnp.einsum('thd,khd->htk', query_heads, key_part, preferred_element_type=...  23.7 us
    lt x12, other arithmetic, block_scores(): block_start + jnp.arange(key_part.shape[0], dtype=jnp.int32) < length  15.6 us
    dynamic_slice x12, local copies, waits for them, and re-layouts, per_device(): lax.scan(running_total, start_state, (key_blocks, block_starts))  15.6 us
    dynamic_update_slice x8, local copies, waits for them, and re-layouts, per_device(): lax.scan(gradient_block, jnp.zeros((row_count, head_count, HEAD_DIM), jnp...  15.5 us
  transfers between devices with their start and end apart: 13, of which 12 were waited for; matrix products, arithmetic and copies ran while one was open for 2% of the time, Pallas kernels for 0%

commit v1 on v0

--- a/solution.py
+++ b/solution.py
@@ -1,3 +1,4 @@
+import functools
 import jax
 import jax.numpy as jnp
 from jax import lax
@@ -7,6 +8,21 @@
 HEAD_DIM = 64
 KERNEL = 32
 GROUPS = 4
+
+
+def columns_produce(xx, dev_axis):
+    return jnp.concatenate(
+        lax.all_to_all(
+            jnp.stack(jnp.split(xx, lax.psum(1, dev_axis), axis=2)),
+            axis_name=dev_axis,
+            split_axis=0,
+            concat_axis=0,
+        ),
+        axis=1,
+    )
+
+
+treat_the_marks = functools.partial(columns_produce, dev_axis="sb")
 
 
 def shifted(x, axis, by):
@@ -40,9 +56,7 @@
     length = lengths[0]
     score_scale = HEAD_DIM ** (-0.5)
     stacked = jnp.stack([queries, keys, values, frames, upstream])
-    mixed = lax.all_to_all(
-        stacked.reshape(5, rows, sub_count, group), "sb", 2, 1, tiled=True
-    ).reshape(5, row_count, group)
+    mixed = treat_the_marks(stacked.reshape(5, rows, sub_count, group)).reshape(5, row_count, group)
     queries_b = mixed[0]
     frames_b = mixed[3]
     upstream_b = mixed[4]

time: 395 us -> 346 us (0.88)
  matrix products: 71.1 us -> 44.1 us
  other arithmetic: 52.1 us -> 37.4 us
  local copies, waits for them, and re-layouts: 59.1 us -> 53.8 us
    dot_general x8, matrix products: 23.7 us -> 7.51 us  [block_scores(): jnp.einsum('thd,khd->htk', query_heads, key_part, preferred_element_type=...]
    dynamic_update_slice x8, local copies, waits for them, and re-layouts: 15.5 us -> 4.42 us  [per_device(): lax.scan(gradient_block, jnp.zeros((row_count, head_count, HEAD_DIM), jnp...]
    reduce_sum x4, other arithmetic: 13.8 us -> 4.17 us  [running_total(): jnp.sum(jnp.exp(scores - higher[:, :, None]), axis=2)]
    dot_general x4, matrix products: 9.72 us -> 2.36 us  [gradient_block(): jnp.einsum('htk,khd->thd', score_grad, key_part, preferred_element_type=j...]
    dynamic_slice x12, local copies, waits for them, and re-layouts: 15.6 us -> 10 us  [per_device(): lax.scan(running_total, start_state, (key_blocks, block_starts))]
  transfers between devices with their start and end apart: 13 -> 13, of which waited for: 12 -> 12; matrix products, arithmetic and copies ran while one was open for 2% -> 3% of each run, Pallas kernels for 0% -> 0%
where the time goes in v1:
time: 346 us; the launch traced here: 345 us
  waiting for transfers between devices  143 us (41%)
  local copies, waits for them, and re-layouts  53.8 us (16%)
  matrix products  44.1 us (13%)
  other arithmetic  37.4 us (11%)
  starting transfers between devices  24.9 us (7%)
  blocking collectives  24.6 us (7%)
  between operations  15.8 us (5%)
    all_gather x1, waiting for transfers between devices, per_device(): lax.all_gather(jnp.concatenate([mixed[1], mixed[2]], axis=1), 'sa', axis=...  47.3 us
    ppermute x8, waiting for transfers between devices, butterfly_sum(): x = x + lax.ppermute(x, axis, [(i, i ^ step) for i in range(count)])  45.5 us
    reduce_scatter x1, waiting for transfers between devices, per_device(): lax.psum_scatter(grad_terms.reshape(span, 2 * group).astype(jnp.bfloat16)...  44.7 us
    all_to_all x1, blocking collectives, columns_produce(): lax.all_to_all(jnp.stack(jnp.split(xx, lax.psum(1, dev_axis), axis=2)), a...  24.6 us
    lt x12, other arithmetic, block_scores(): block_start + jnp.arange(key_part.shape[0], dtype=jnp.int32) < length  15.4 us
    ppermute x8, starting transfers between devices, butterfly_sum(): x = x + lax.ppermute(x, axis, [(i, i ^ step) for i in range(count)])  14.4 us
    dot_general x4, matrix products, score_grads(): jnp.einsum('thd,khd->htk', grad_heads, value_part, preferred_element_type...  10.8 us
    dot_general x4, matrix products, attend_block(): jnp.einsum('htk,khd->thd', prob_bf, value_part, preferred_element_type=jn...  10.8 us
  transfers between devices with their start and end apart: 13, of which 12 were waited for; matrix products, arithmetic and copies ran while one was open for 3% of the time, Pallas kernels for 0%

profile of v1, /device:TPU:2, one launch (start us, length us, event | category | flops | bytes accessed | tf_op | source)
XLA Modules:
  0.0 344.6 jit_solution(11747614028367697863)
XLA Ops:
  7.2 1.3 stack.148
  8.5 1.3 stack.149
  9.8 1.3 stack.150
  11.1 1.3 stack.151
  13.3 3.3 fusion.114
  17.4 24.6 %all_to_all.20 = bf16[4,5,160,1,192]{4,2,1,3,0:T(8,128)(2,1)S(1)} all-to-all(bf16[4,5,160,1,192]{4,2,1,3,0:T(8,128)(2,1)S(1)} %pad_maximum_fusion), channel_id=1, replica_groups=mesh['dp'=16,'sa'=4,'sb'=4] {'sb'}, dimensions={0} | all-to-all | bytes 2457600 | tf_op jit(solution)/shard_map/all_to_all | solution.py:15
  47.3 47.3 %all-gather.2.cloned.1.call-done = bf16[2560,384]{1,0:T(8,128)(2,1)} async-done(((bf16[640,384]{1,0:T(8,128)(2,1)}), bf16[2560,384]{1,0:T(8,128)(2,1)}) %all-gather.2.cloned.1.call-update) | async-done | bytes 1966096 | tf_op jit(solution)/shard_map/all_gather | solution.py:63
  94.7 3.4 fusion.111
  98.1 1.6 copy.110
  100.0 18.6 %while.37 = (s32[]{:T(128)}, f32[3,640]{1,0:T(4,128)S(1)}, f32[3,640]{1,0:T(4,128)S(1)}, s32[4]{0:T(128)}, s32[]{:T(128)}, /*index=5*/bf16[4,640,3,64]{1,3,2,0:T...) while((s32[]{:T(128)}, f32[3,640]{1,0:T(4,128)S(1)}, f32[3,640]{1,0:T(4,128)S(1)}, ...), condition=%wide.region_3.4_spmd.clone, body=%wide.region_0.3_spmd.clone.sunk | while | flops 165898880 | bytes 10424200 | solution.py:95
  100.0 1.2 dynamic_slice.76
  101.3 1.3 add_compare_fusion.7
  104.7 1.2 dynamic_slice.76
  105.9 1.3 add_compare_fusion.7
  109.3 1.2 dynamic_slice.76
  110.5 1.3 add_compare_fusion.7
  114.0 1.2 dynamic_slice.76
  115.2 1.3 add_compare_fusion.7
  120.6 18.8 %while.38 = (s32[]{:T(128)}, f32[640,3,64]{0,2,1:T(8,128)S(1)}, bf16[4,640,3,64]{1,3,2,0:T(8,128)(2,1)}, s32[4]{0:T(128)S(1)}, s32[]{:T(128)}, /*index=5*/bf16[4...) while((s32[]{:T(128)}, f32[640,3,64]{0,2,1:T(8,128)S(1)}, ...), condition=%wide.region_5.6_spmd.clone, body=%wide.region_4.5_spmd.clone.sunk | while | flops 319735040 | bytes 1733898 | solution.py:111
  121.2 1.3 add_compare_fusion.8
  122.6 2.7 fusion.152
  125.9 1.3 add_compare_fusion.8
  127.3 2.7 fusion.152
  130.6 1.3 add_compare_fusion.8
  132.0 2.7 fusion.152
  135.3 1.3 add_compare_fusion.8
  136.7 2.7 fusion.152
  140.4 1.3 copy.115
  141.9 5.3 %collective-permute-start = (bf16[31,192]{1,0:T(8,128)(2,1)S(1)}, bf16[31,192]{1,0:T(8,128)(2,1)S(1)}, u32[]{:S(2)}, u32[]{:S(2)}) collective-permute-start(bf16[31,192]{1,0:T(8,128)(2,1)S(1)} %slice.531), channel_id=1, source_target_pairs={{0,4},{4,8},{8,12},{1,5},{5,9},{9,13},{2,6},{6,10},{10,14},{3,7},{... | collective-permute-start | bytes 35720 | tf_op jit(solution)/shard_map/ppermute | solution.py:31
  148.7 7.1 %fusion.71 = (f32[192]{0:T(256)}, f32[192]{0:T(256)}, f32[192]{0:T(256)}, f32[192]{0:T(256)}, f32[192]{0:T(256)}, /*index=5*/f32[192]{0:T(256)}, f32[192]{0:T(25...) fusion(f32[671,192]{1,0:T(8,128)S(1)} %maximum_convert_fusion, ...), kind=kLoop, calls=%fused_computation.114 | loop fusion | flops 13636224 | bytes 16750720 | tf_op jit(solution)/shard_map/reduce_sum | solution.py:139
  155.8 1.3 collective-permute-start.1
  157.1 5.6 %collective-permute-done.1 = bf16[31,192]{1,0:T(8,128)(2,1)S(1)} collective-permute-done((bf16[31,192]{1,0:T(8,128)(2,1)S(1)}, bf16[31,192]{1,0:T(8,128)(2,1)S(1)}, u32[]{:S(2)}, u32[]{:S(2)}) %collective-permute-start.1) | collective-permute-done | bytes 11936 | tf_op jit(solution)/shard_map/ppermute | solution.py:31
  162.8 3.1 fusion.75
  166.8 1.2 multiply_reduce_fusion
  168.1 41.5 %while.39 = (s32[]{:T(128)}, f32[640,3,64]{0,2,1:T(8,128)S(1)}, bf16[4,640,384]{2,1,0:T(8,128)(2,1)}, bf16[4,640,3,64]{1,3,2,0:T(8,128)(2,1)S(1)}, s32[4]{0:T(12...) while((s32[]{:T(128)}, f32[640,3,64]{0,2,1:T(8,128)S(1)}, ...), condition=%wide.region_8.9_spmd.clone, body=%wide.region_7.8_spmd.clone.sunk | while | flops 800195840 | bytes 28287540 | solution.py:184
  168.7 1.3 add_compare_fusion.9
  170.9 2.3 fusion.165
  173.1 2.7 multiply_convert_fusion.3
  179.1 1.3 add_compare_fusion.9
  181.2 2.3 fusion.165
  183.5 2.7 multiply_convert_fusion.3
  189.5 1.3 add_compare_fusion.9
  191.6 2.2 fusion.165
  193.9 2.7 multiply_convert_fusion.3
  199.9 1.3 add_compare_fusion.9
  202.0 2.3 fusion.165
  204.2 2.7 multiply_convert_fusion.3
  213.4 44.7 %reduce-scatter.2.cloned.1.call-done = bf16[640,384]{1,0:T(8,128)(2,1)} async-done(((bf16[2560,384]{1,0:T(8,128)(2,1)}), bf16[640,384]{1,0:T(8,128)(2,1)}) %reduce-scatter.2.cloned.1.call-update) | async-done | bytes 491536 | tf_op jit(solution)/shard_map/reduce_scatter | solution.py:189
  261.5 2.7 copy.121
  264.3 3.9 %all-to-all-start.1 = ((bf16[5,4,160,1,192]{4,2,3,0,1:T(8,128)(2,1)}), bf16[5,4,160,1,192]{4,2,3,0,1:T(8,128)(2,1)S(1)}, u32[]{:S(2)}, u32[]{:S(2)}) async-start(bf16[5,4,160,1,192]{4,2,3,0,1:T(8,128)(2,1)} %copy.121), calls=%async_computation.2 | async-start | bytes 3276800 | tf_op jit(solution)/shard_map/all_to_all | solution.py:204
  270.3 2.0 collective-permute-start.2
  272.2 17.9 %collective-permute-done.2 = f32[32,768]{1,0:T(8,128)S(1)} collective-permute-done((f32[32,768]{1,0:T(8,128)S(1)}, f32[32,768]{1,0:T(8,128)S(1)}, u32[]{:S(2)}, u32[]{:S(2)}) %collective-permute-start.2) | collective-permute-done | bytes 98336 | tf_op jit(solution)/shard_map/ppermute | solution.py:39
  290.7 1.5 collective-permute-start.3
  292.2 3.2 collective-permute-done.3
  295.4 2.5 collective-permute-start.4
  297.9 4.4 %collective-permute-done.4 = f32[32,768]{1,0:T(8,128)S(1)} collective-permute-done((f32[32,768]{1,0:T(8,128)S(1)}, f32[32,768]{1,0:T(8,128)S(1)}, u32[]{:S(2)}, u32[]{:S(2)}) %collective-permute-start.4) | collective-permute-done | bytes 98336 | tf_op jit(solution)/shard_map/ppermute | solution.py:39
  302.3 2.6 collective-permute-start.5
  304.9 7.1 %collective-permute-done.5 = f32[32,768]{1,0:T(8,128)S(1)} collective-permute-done((f32[32,768]{1,0:T(8,128)S(1)}, f32[32,768]{1,0:T(8,128)S(1)}, u32[]{:S(2)}, u32[]{:S(2)}) %collective-permute-start.5) | collective-permute-done | bytes 98336 | tf_op jit(solution)/shard_map/ppermute | solution.py:39
  312.1 1.3 collective-permute-done.6
  313.4 3.1 collective-permute-start.7
  316.5 3.4 collective-permute-done.7
  320.5 4.1 %collective-permute-done.8 = f32[32,768]{1,0:T(8,128)S(1)} collective-permute-done((f32[32,768]{1,0:T(8,128)S(1)}, f32[32,768]{1,0:T(8,128)S(1)}, u32[]{:S(2)}, u32[]{:S(2)}) %collective-permute-start.8) | collective-permute-done | bytes 98336 | tf_op jit(solution)/shard_map/ppermute | solution.py:39
  324.6 2.1 collective-permute-start.9
  326.6 4.1 %collective-permute-done.9 = f32[32,768]{1,0:T(8,128)S(1)} collective-permute-done((f32[32,768]{1,0:T(8,128)S(1)}, f32[32,768]{1,0:T(8,128)S(1)}, u32[]{:S(2)}, u32[]{:S(2)}) %collective-permute-start.9) | collective-permute-done | bytes 98336 | tf_op jit(solution)/shard_map/ppermute | solution.py:39
  (234 shorter events, 56.6 us)
Async XLA Ops:
  7.2 5.1 %copy-start.12 = (bf16[160,768]{1,0:T(8,128)(2,1)S(1)}, bf16[160,768]{1,0:T(8,128)(2,1)}, u32[]{:S(2)}) copy-start(bf16[160,768]{1,0:T(8,128)(2,1)} %param.17) | copy-start | bytes 737284
  7.2 87.5 %all-gather.2.cloned.1.call-start = ((), (), s32[]{:S(2)}) async-start(), calls=%async_computation.3 | async-start | bytes 2457600 | tf_op jit(solution)/shard_map/all_gather | solution.py:63
  44.1 214.0 %reduce-scatter.2.cloned.1.call-start = ((), (), s32[]{:S(2)}) async-start(), calls=%async_computation.4 | async-start | bytes 2457600 | tf_op jit(solution)/shard_map/reduce_scatter | solution.py:189
  46.1 51.9 %copy-start.13 = (f32[32,192]{1,0:T(8,128)}, f32[32,192]{1,0:T(8,128)S(1)}, u32[]{:S(2)}) copy-start(f32[32,192]{1,0:T(8,128)S(1)} %dynamic-slice_convert_fusion) | copy-start | bytes 73732
  119.4 1.1 copy-start.10
  119.4 1.1 copy-start.50
  139.4 9.1 %copy-start.11 = (f32[640,3,64]{0,2,1:T(8,128)}, f32[640,3,64]{0,2,1:T(8,128)S(1)}, u32[]{:S(2)}) copy-start(f32[640,3,64]{0,2,1:T(8,128)S(1)} %get-tuple-element.146) | copy-start | bytes 1474564
  139.4 2.3 copy-start.4
  140.2 8.3 %copy-start.8 = (bf16[1,4,160,1,192]{4,2,0,3,1:T(8,128)(2,1)S(1)}, bf16[1,4,160,1,192]{4,2,0,3,1:T(8,128)(2,1)}, u32[]{:S(2)}) copy-start(bf16[1,4,160,1,192]{4,2,0,3,1:T(8,128)(2,1)} %get-tuple-element.495) | copy-start | bytes 737284
  140.2 8.3 %copy-start.14 = (f32[1,192]{1,0:T(1,128)S(1)}, f32[1,192]{1,0:T(1,128)}, u32[]{:S(2)}) copy-start(f32[1,192]{1,0:T(1,128)} %get-tuple-element.507) | copy-start | bytes 2308
  140.2 8.3 %copy-start.15 = (f32[1,192]{1,0:T(1,128)S(1)}, f32[1,192]{1,0:T(1,128)}, u32[]{:S(2)}) copy-start(f32[1,192]{1,0:T(1,128)} %get-tuple-element.508) | copy-start | bytes 2308
  140.2 8.3 %copy-start.16 = (f32[1,192]{1,0:T(1,128)S(1)}, f32[1,192]{1,0:T(1,128)}, u32[]{:S(2)}) copy-start(f32[1,192]{1,0:T(1,128)} %get-tuple-element.509) | copy-start | bytes 2308
  140.2 8.3 %copy-start.17 = (f32[1,192]{1,0:T(1,128)S(1)}, f32[1,192]{1,0:T(1,128)}, u32[]{:S(2)}) copy-start(f32[1,192]{1,0:T(1,128)} %get-tuple-element.510) | copy-start | bytes 2308
  140.3 8.3 %copy-start.18 = (f32[1,192]{1,0:T(1,128)S(1)}, f32[1,192]{1,0:T(1,128)}, u32[]{:S(2)}) copy-start(f32[1,192]{1,0:T(1,128)} %get-tuple-element.511) | copy-start | bytes 2308
  140.3 8.3 %copy-start.19 = (f32[1,192]{1,0:T(1,128)S(1)}, f32[1,192]{1,0:T(1,128)}, u32[]{:S(2)}) copy-start(f32[1,192]{1,0:T(1,128)} %get-tuple-element.512) | copy-start | bytes 2308
  140.3 8.3 %copy-start.20 = (f32[1,192]{1,0:T(1,128)S(1)}, f32[1,192]{1,0:T(1,128)}, u32[]{:S(2)}) copy-start(f32[1,192]{1,0:T(1,128)} %get-tuple-element.513) | copy-start | bytes 2308
  140.3 8.3 %copy-start.21 = (f32[1,192]{1,0:T(1,128)S(1)}, f32[1,192]{1,0:T(1,128)}, u32[]{:S(2)}) copy-start(f32[1,192]{1,0:T(1,128)} %get-tuple-element.514) | copy-start | bytes 2308
  140.3 8.3 %copy-start.22 = (f32[1,192]{1,0:T(1,128)S(1)}, f32[1,192]{1,0:T(1,128)}, u32[]{:S(2)}) copy-start(f32[1,192]{1,0:T(1,128)} %get-tuple-element.515) | copy-start | bytes 2308
  140.3 8.3 %copy-start.23 = (f32[1,192]{1,0:T(1,128)S(1)}, f32[1,192]{1,0:T(1,128)}, u32[]{:S(2)}) copy-start(f32[1,192]{1,0:T(1,128)} %get-tuple-element.516) | copy-start | bytes 2308
  140.3 8.3 %copy-start.24 = (f32[1,192]{1,0:T(1,128)S(1)}, f32[1,192]{1,0:T(1,128)}, u32[]{:S(2)}) copy-start(f32[1,192]{1,0:T(1,128)} %get-tuple-element.517) | copy-start | bytes 2308
  140.3 8.3 %copy-start.25 = (f32[1,192]{1,0:T(1,128)S(1)}, f32[1,192]{1,0:T(1,128)}, u32[]{:S(2)}) copy-start(f32[1,192]{1,0:T(1,128)} %get-tuple-element.518) | copy-start | bytes 2308
  140.3 8.3 %copy-start.26 = (f32[1,192]{1,0:T(1,128)S(1)}, f32[1,192]{1,0:T(1,128)}, u32[]{:S(2)}) copy-start(f32[1,192]{1,0:T(1,128)} %get-tuple-element.519) | copy-start | bytes 2308
  140.3 8.3 %copy-start.27 = (f32[1,192]{1,0:T(1,128)S(1)}, f32[1,192]{1,0:T(1,128)}, u32[]{:S(2)}) copy-start(f32[1,192]{1,0:T(1,128)} %get-tuple-element.520) | copy-start | bytes 2308
  140.4 8.3 %copy-start.28 = (f32[1,192]{1,0:T(1,128)S(1)}, f32[1,192]{1,0:T(1,128)}, u32[]{:S(2)}) copy-start(f32[1,192]{1,0:T(1,128)} %get-tuple-element.521) | copy-start | bytes 2308
  140.4 8.3 %copy-start.29 = (f32[1,192]{1,0:T(1,128)S(1)}, f32[1,192]{1,0:T(1,128)}, u32[]{:S(2)}) copy-start(f32[1,192]{1,0:T(1,128)} %get-tuple-element.522) | copy-start | bytes 2308
  140.4 8.3 %copy-start.30 = (f32[1,192]{1,0:T(1,128)S(1)}, f32[1,192]{1,0:T(1,128)}, u32[]{:S(2)}) copy-start(f32[1,192]{1,0:T(1,128)} %get-tuple-element.523) | copy-start | bytes 2308
  140.4 8.3 %copy-start.31 = (f32[1,192]{1,0:T(1,128)S(1)}, f32[1,192]{1,0:T(1,128)}, u32[]{:S(2)}) copy-start(f32[1,192]{1,0:T(1,128)} %get-tuple-element.524) | copy-start | bytes 2308
  141.7 6.4 %copy-start = (f32[640,192]{1,0:T(8,128)}, f32[640,192]{1,0:T(8,128)S(1)}, u32[]{:S(2)}) copy-start(f32[640,192]{1,0:T(8,128)S(1)} %copy.115) | copy-start | bytes 1474564
  141.9 6.5 %collective-permute-start = (bf16[31,192]{1,0:T(8,128)(2,1)S(1)}, bf16[31,192]{1,0:T(8,128)(2,1)S(1)}, u32[]{:S(2)}, u32[]{:S(2)}) collective-permute-start(bf16[31,192]{1,0:T(8,128)(2,1)S(1)} %slice.531), channel_id=1, source_target_pairs={{0,4},{4,8},{8,12},{1,5},{5,9},{9,13},{2,6},{6,10},{10,14},{3,7},{... | collective-permute-start | bytes 35720 | tf_op jit(solution)/shard_map/ppermute | solution.py:31
  155.8 10.1 %copy-start.2 = (bf16[640,192]{1,0:T(8,128)(2,1)}, bf16[640,192]{1,0:T(8,128)(2,1)S(1)}, u32[]{:S(2)}) copy-start(bf16[640,192]{1,0:T(8,128)(2,1)S(1)} %get-tuple-element.484) | copy-start | bytes 737284
  155.8 6.9 %collective-permute-start.1 = (bf16[31,192]{1,0:T(8,128)(2,1)S(1)}, bf16[31,192]{1,0:T(8,128)(2,1)S(1)}, u32[]{:S(2)}, u32[]{:S(2)}) collective-permute-start(bf16[31,192]{1,0:T(8,128)(2,1)S(1)} %slice.596), channel_id=1, source_target_pairs={{4,0},{8,4},{12,8},{5,1},{9,5},{13,9},{6,2},{10,6},{14,10},{7,3},{... | collective-permute-start | bytes 35720 | tf_op jit(solution)/shard_map/ppermute | solution.py:31
  162.8 5.3 %copy-start.51 = (s32[4]{0:T(128)S(1)}, s32[4]{0:T(128)}, u32[]{:S(2)}) copy-start(s32[4]{0:T(128)} %get-tuple-element.838) | copy-start | bytes 52
  166.0 2.1 copy-start.6
  209.6 1.2 copy-start.5
  209.6 1.4 copy-start.9
  212.3 48.5 %copy-start.7 = (bf16[640,192]{1,0:T(8,128)(2,1)S(1)}, bf16[640,192]{1,0:T(8,128)(2,1)}, u32[]{:S(2)}) copy-start(bf16[640,192]{1,0:T(8,128)(2,1)} %copy-done.6) | copy-start | bytes 737284
  264.3 3.9 %copy-start.3 = (bf16[640,192]{1,0:T(8,128)(2,1)S(1)}, bf16[640,192]{1,0:T(8,128)(2,1)}, u32[]{:S(2)}) copy-start(bf16[640,192]{1,0:T(8,128)(2,1)} %copy-done.2) | copy-start | bytes 737284
  264.3 67.2 %all-to-all-start.1 = ((bf16[5,4,160,1,192]{4,2,3,0,1:T(8,128)(2,1)}), bf16[5,4,160,1,192]{4,2,3,0,1:T(8,128)(2,1)S(1)}, u32[]{:S(2)}, u32[]{:S(2)}) async-start(bf16[5,4,160,1,192]{4,2,3,0,1:T(8,128)(2,1)} %copy.121), calls=%async_computation.2 | async-start | bytes 3276800 | tf_op jit(solution)/shard_map/all_to_all | solution.py:204
  268.2 1.3 copy-start.32
  268.2 1.3 copy-start.33
  268.2 1.3 copy-start.34
  268.2 1.3 copy-start.35
  268.3 1.3 copy-start.36
  268.3 1.3 copy-start.37
  268.3 1.3 copy-start.38
  268.3 1.3 copy-start.39
  268.3 1.3 copy-start.40
  268.3 1.3 copy-start.41
  268.3 1.3 copy-start.42
  268.3 1.3 copy-start.43
  268.3 1.3 copy-start.44
  268.3 1.3 copy-start.45
  268.4 1.3 copy-start.46
  268.4 1.3 copy-start.47
  268.4 1.3 copy-start.48
  268.4 1.3 copy-start.49
  270.3 19.9 %collective-permute-start.2 = (f32[32,768]{1,0:T(8,128)S(1)}, f32[32,768]{1,0:T(8,128)S(1)}, u32[]{:S(2)}, u32[]{:S(2)}) collective-permute-start(f32[32,768]{1,0:T(8,128)S(1)} %dynamic_update_slice.9), channel_id=1, source_target_pairs={{0,1},{1,0},{2,3},{3,2},{4,5},{5,4},{6,7},{7,6},{8,9},{9,8},{10,11... | collective-permute-start | bytes 294920 | tf_op jit(solution)/shard_map/ppermute | solution.py:39
  290.7 4.7 %collective-permute-start.3 = (f32[32,768]{1,0:T(8,128)S(1)}, f32[32,768]{1,0:T(8,128)S(1)}, u32[]{:S(2)}, u32[]{:S(2)}) collective-permute-start(f32[32,768]{1,0:T(8,128)S(1)} %add.364), channel_id=1, source_target_pairs={{0,2},{1,3},{2,0},{3,1},{4,6},{5,7},{6,4},{7,5},{8,10},{9,11},{10,... | collective-permute-start | bytes 294920 | tf_op jit(solution)/shard_map/ppermute | solution.py:39
  295.4 6.8 %collective-permute-start.4 = (f32[32,768]{1,0:T(8,128)S(1)}, f32[32,768]{1,0:T(8,128)S(1)}, u32[]{:S(2)}, u32[]{:S(2)}) collective-permute-start(f32[32,768]{1,0:T(8,128)S(1)} %add.365), channel_id=1, source_target_pairs={{0,4},{4,0},{8,12},{12,8},{1,5},{5,1},{9,13},{13,9},{2,6},{6,2},{1... | collective-permute-start | bytes 294920 | tf_op jit(solution)/shard_map/ppermute | solution.py:39
  302.3 9.7 %collective-permute-start.5 = (f32[32,768]{1,0:T(8,128)S(1)}, f32[32,768]{1,0:T(8,128)S(1)}, u32[]{:S(2)}, u32[]{:S(2)}) collective-permute-start(f32[32,768]{1,0:T(8,128)S(1)} %add.366), channel_id=1, source_target_pairs={{0,8},{4,12},{8,0},{12,4},{1,9},{5,13},{9,1},{13,5},{2,10},{6,14},... | collective-permute-start | bytes 294920 | tf_op jit(solution)/shard_map/ppermute | solution.py:39
  312.0 1.4 collective-permute-start.6
  313.4 6.4 %collective-permute-start.7 = (f32[32,768]{1,0:T(8,128)S(1)}, f32[32,768]{1,0:T(8,128)S(1)}, u32[]{:S(2)}, u32[]{:S(2)}) collective-permute-start(f32[32,768]{1,0:T(8,128)S(1)} %add.368), channel_id=1, source_target_pairs={{0,32},{16,48},{32,0},{48,16},{64,96},{80,112},{96,64},{112,80},{1... | collective-permute-start | bytes 294920 | tf_op jit(solution)/shard_map/ppermute | solution.py:39
  319.8 4.7 %collective-permute-start.8 = (f32[32,768]{1,0:T(8,128)S(1)}, f32[32,768]{1,0:T(8,128)S(1)}, u32[]{:S(2)}, u32[]{:S(2)}) collective-permute-start(f32[32,768]{1,0:T(8,128)S(1)} %add.369), channel_id=1, source_target_pairs={{0,64},{16,80},{32,96},{48,112},{64,0},{80,16},{96,32},{112,48},{1... | collective-permute-start | bytes 294920 | tf_op jit(solution)/shard_map/ppermute | solution.py:39
  324.6 6.2 %collective-permute-start.9 = (f32[32,768]{1,0:T(8,128)S(1)}, f32[32,768]{1,0:T(8,128)S(1)}, u32[]{:S(2)}, u32[]{:S(2)}) collective-permute-start(f32[32,768]{1,0:T(8,128)S(1)} %add.370), channel_id=1, source_target_pairs={{0,128},{16,144},{32,160},{48,176},{64,192},{80,208},{96,224},{112... | collective-permute-start | bytes 294920 | tf_op jit(solution)/shard_map/ppermute | solution.py:39
  (1 other events, 1.1 us)
Sparse Core Ops, SparseCore 0:
  44.2 50.4 all-gather.1
  209.8 48.2 reduce-scatter.1
